TPU v7x, 256 devices: a whole 4x4x8 slice. The times are simulated.
256 devices in a mesh: dp: 4 (over x), expert: 64 (over y, z, core).
Axes of the slice: x: 4, y: 4, z: 8, core: 2. Of those that a mesh axis runs over, the one named last changes fastest.
Arguments:
- features: bfloat16 [65536, 512], P(('dp', 'expert')), may hold values from -6 to 6
- slots: int32 [65536], P(('dp', 'expert')), may hold values from 0 to 31
- routes: int32 [65536, 2], P(('dp', 'expert')), may hold values from 0 to 63, all different within a row; in each aligned block of 256 rows (0 to 255, 256 to 511, ...) at most 16 rows name the same one
- cotangent: bfloat16 [65536, 512], P(('dp', 'expert')), may hold values from -1.5 to 1.5
- pos_table: bfloat16 [32, 64], replicated, may hold values from -6 to 6
- tower_in: bfloat16 [64, 256], replicated, may hold values from -0.75 to 0.75
- tower_out: bfloat16 [256, 512], replicated, may hold values from -0.375 to 0.375
- router: bfloat16 [512, 64], replicated, may hold values from -0.5 to 0.5
- w_up: bfloat16 [64, 512, 2048], P('expert'), may hold values from -0.25 to 0.25
- w_down: bfloat16 [64, 2048, 512], P('expert'), may hold values from -0.125 to 0.125
Outputs:
- layer_out: bfloat16 [65536, 512], P(('dp', 'expert'))
- grad_in: bfloat16 [65536, 512], P(('dp', 'expert'))
- grad_up: bfloat16 [64, 512, 2048], P('expert')
- grad_down: bfloat16 [64, 2048, 512], P('expert')
Inputs may be any that keep to these rules, and one draw needn't show every extreme that they name: `routes`: within the rows of one device no expert is named by more than 16 rows; in some devices' rows one expert is named by exactly 16.
All inputs are finite; a program needn't handle non-finite values.
Results may differ from a plain program's by a relative error of at most 0.013.
Values may be sent and summed in bfloat16 or wider, within the bound.
No kernel may reach another device: no remote copies, remote signals or barrier semaphores. Data moves between devices by JAX's collectives and lax.ppermute only.
A program may use at most 128 MiB of HBM per device.

v0:
```python
import jax
import jax.numpy as jnp
from jax import lax
from jax.sharding import PartitionSpec as P

TOP = 2
coef_a = 0.7978845608028654
coef_b = 0.044715


def gelu_pair(pre_act):
    inner = coef_a * (pre_act + coef_b * pre_act * pre_act * pre_act)
    tanh_val = jnp.tanh(inner)
    activated = 0.5 * pre_act * (1.0 + tanh_val)
    gelu_slope = 0.5 * (1.0 + tanh_val) + 0.5 * pre_act * (1.0 - tanh_val * tanh_val) * coef_a * (
        1.0 + 3.0 * coef_b * pre_act * pre_act
    )
    return (activated, gelu_slope)


def contract_rows(left, right):
    return lax.dot_general(
        left, right, (((0,), (0,)), ((), ())), preferred_element_type=jnp.float32
    )


def contract_cols(left, right):
    return lax.dot_general(
        left, right, (((1,), (1,)), ((), ())), preferred_element_type=jnp.float32
    )


def expert_forward(flat_in, w_up_one, w_down_one):
    pre_act = jnp.dot(flat_in, w_up_one, preferred_element_type=jnp.float32)
    activated, gelu_slope = gelu_pair(pre_act)
    hidden = activated.astype(jnp.bfloat16)
    outputs = jnp.dot(hidden, w_down_one, preferred_element_type=jnp.float32).astype(jnp.bfloat16)
    return (hidden, gelu_slope, outputs)


def expert_backward(flat_in, flat_cot, hidden, gelu_slope, w_up_one, w_down_one):
    grad_down_part = contract_rows(hidden, flat_cot)
    d_hidden = contract_cols(flat_cot, w_down_one)
    d_pre = (d_hidden * gelu_slope).astype(jnp.bfloat16)
    d_inputs = contract_cols(d_pre, w_up_one).astype(jnp.bfloat16)
    grad_up_part = contract_rows(flat_in, d_pre)
    sum_up, sum_down = (
        lax.psum(grad_up_part.astype(jnp.bfloat16), "dp").astype(jnp.float32),
        lax.psum(grad_down_part.astype(jnp.bfloat16), "dp").astype(jnp.float32),
    )
    return (d_inputs, sum_up, sum_down)


def per_device(
    features, slots, routes, cotangent, pos_table, tower_in, tower_out, router, w_up, w_down
):
    tok_rows = features.shape[0]
    feature_width = features.shape[1]
    n_experts = router.shape[1]
    capacity = 2 * TOP * tok_rows // n_experts
    pos_hidden = jax.nn.relu(jnp.dot(pos_table, tower_in, preferred_element_type=jnp.float32))
    pos_rows = jnp.dot(pos_hidden, tower_out.astype(jnp.float32), precision=lax.Precision.HIGHEST)
    slot_hot = (slots[:, None] == jnp.arange(pos_table.shape[0], dtype=jnp.int32)[None, :]).astype(
        jnp.float32
    )
    pos_feats = jnp.dot(slot_hot, pos_rows, precision=lax.Precision.HIGHEST)
    mixed_in = (features.astype(jnp.float32) + pos_feats).astype(jnp.bfloat16)
    logits = jnp.dot(mixed_in, router, preferred_element_type=jnp.float32)
    expert_ids = jnp.arange(n_experts, dtype=jnp.int32)
    route_hot = routes[:, :, None] == expert_ids[None, None, :]
    chosen = jnp.sum(jnp.where(route_hot, logits[:, None, :], 0.0), axis=2)
    squashed = 1.0 / (1.0 + jnp.exp(-chosen))
    gate_total = jnp.sum(squashed, axis=1, keepdims=True)
    gates = squashed / gate_total
    cot_wide = cotangent.astype(jnp.float32)
    slot_cot = (gates[:, :, None] * cot_wide[:, None, :]).astype(jnp.bfloat16)
    flat_routes = routes.reshape(-1)
    flat_hot = route_hot.reshape(-1, n_experts).astype(jnp.int32)
    before = jnp.cumsum(flat_hot, axis=0, dtype=jnp.int32) - flat_hot
    slot_rank = jnp.sum(before * flat_hot, axis=1, dtype=jnp.int32)
    slot_place = flat_routes * capacity + slot_rank
    buffer_shape = (n_experts, capacity, feature_width)
    send_in = (
        jnp.zeros((n_experts * capacity, feature_width), jnp.bfloat16)
        .at[slot_place]
        .set(jnp.repeat(mixed_in, TOP, axis=0))
        .reshape(buffer_shape)
    )
    send_cot = (
        jnp.zeros((n_experts * capacity, feature_width), jnp.bfloat16)
        .at[slot_place]
        .set(slot_cot.reshape(-1, feature_width))
        .reshape(buffer_shape)
    )
    w_up_one = w_up[0]
    w_down_one = w_down[0]
    recv_in = lax.all_to_all(send_in, "expert", split_axis=0, concat_axis=0, tiled=True)
    flat_in = recv_in.reshape(-1, feature_width)
    hidden, gelu_slope, outputs = expert_forward(flat_in, w_up_one, w_down_one)
    back_out = lax.all_to_all(
        outputs.reshape(buffer_shape), "expert", split_axis=0, concat_axis=0, tiled=True
    )
    recv_cot = lax.all_to_all(send_cot, "expert", split_axis=0, concat_axis=0, tiled=True)
    flat_cot = recv_cot.reshape(-1, feature_width)
    d_inputs, sum_up, sum_down = expert_backward(
        flat_in, flat_cot, hidden, gelu_slope, w_up_one, w_down_one
    )
    back_grad = lax.all_to_all(
        d_inputs.reshape(buffer_shape), "expert", split_axis=0, concat_axis=0, tiled=True
    )
    expert_out = back_out.reshape(-1, feature_width)[slot_place].reshape(
        tok_rows, TOP, feature_width
    )
    slot_grad = back_grad.reshape(-1, feature_width)[slot_place].reshape(
        tok_rows, TOP, feature_width
    )
    expert_wide = expert_out.astype(jnp.float32)
    layer_out = (
        mixed_in.astype(jnp.float32) + jnp.sum(gates[:, :, None] * expert_wide, axis=1)
    ).astype(jnp.bfloat16)
    d_gates = jnp.sum(expert_wide * cot_wide[:, None, :], axis=2)
    mean_term = jnp.sum(gates * d_gates, axis=1, keepdims=True)
    d_chosen = (d_gates - mean_term) / gate_total * squashed * (1.0 - squashed)
    d_logits = jnp.sum(jnp.where(route_hot, d_chosen[:, :, None], 0.0), axis=1)
    d_router = lax.dot_general(
        d_logits,
        router.astype(jnp.float32),
        (((1,), (1,)), ((), ())),
        precision=lax.Precision.HIGHEST,
    )
    grad_in = (cot_wide + jnp.sum(slot_grad.astype(jnp.float32), axis=1) + d_router).astype(
        jnp.bfloat16
    )
    return (
        layer_out,
        grad_in,
        sum_up.astype(jnp.bfloat16)[None],
        sum_down.astype(jnp.bfloat16)[None],
    )


def solution(mesh):
    return jax.shard_map(
        per_device,
        mesh=mesh,
        in_specs=(
            P(("dp", "expert"), None),
            P(("dp", "expert")),
            P(("dp", "expert"), None),
            P(("dp", "expert"), None),
            P(),
            P(),
            P(),
            P(),
            P("expert", None, None),
            P("expert", None, None),
        ),
        out_specs=(
            P(("dp", "expert"), None),
            P(("dp", "expert"), None),
            P("expert", None, None),
            P("expert", None, None),
        ),
        check_vma=False,
    )
```

profile of v0, /device:TPU:1, one launch (start us, length us, event | category | flops | bytes accessed | tf_op | source)
XLA Modules:
  0.0 234.4 jit_solution(15027040676049464937)
XLA Ops:
  15.0 3.5 %scatter_custom_fusion = bf16[1024,512]{1,0:T(8,128)(2,1)} fusion(s32[512]{0:T(512)S(1)} %bitcast.70, bf16[512,512]{1,0:T(8,128)(2,1)S(1)} %reshape.212, bf16[]{:T(256)} %constant.12.clone.1), kind=kCustom, calls=%fused_computation.39 | custom fusion | bytes 1048578 | tf_op jit(solution)/shard_map/scatter | solution.py:86
  18.5 13.3 %all-to-all-start = ((bf16[64,16,512]{2,1,0:T(8,128)(2,1)}), bf16[64,16,512]{2,1,0:T(8,128)(2,1)}, u32[]{:S(2)}, u32[]{:S(2)}) async-start(bf16[64,16,512]{2,1,0:T(8,128)(2,1)} %bitcast.3), calls=%async_computation | async-start | bytes 2097152 | tf_op jit(solution)/shard_map/all_to_all | solution.py:97
  37.4 4.3 %scatter_custom_fusion.1 = bf16[1024,512]{1,0:T(8,128)(2,1)} fusion(s32[512]{0:T(512)S(1)} %bitcast.71, f32[512,512]{1,0:T(8,128)} %mul.134, f32[512]{0:T(512)S(1)} %reshape.190, bf16[]{:T(256)} %constant.12.clone.1), kind=kCustom, calls=%fused_computation.35 | custom fusion | flops 524288 | bytes 2099202 | tf_op jit(solution)/shard_map/scatter | solution.py:92
  41.7 18.6 %all-to-all-done = bf16[64,16,512]{2,1,0:T(8,128)(2,1)} async-done(((bf16[64,16,512]{2,1,0:T(8,128)(2,1)}), bf16[64,16,512]{2,1,0:T(8,128)(2,1)}, u32[]{:S(2)}, u32[]{:S(2)}) %all-to-all-start) | async-done | bytes 1048608 | tf_op jit(solution)/shard_map/all_to_all | solution.py:97
  60.3 6.2 %all-to-all-start.2 = ((bf16[64,16,512]{2,1,0:T(8,128)(2,1)}), bf16[64,16,512]{2,1,0:T(8,128)(2,1)S(1)}, u32[]{:S(2)}, u32[]{:S(2)}) async-start(bf16[64,16,512]{2,1,0:T(8,128)(2,1)} %bitcast.9), calls=%async_computation.2 | async-start | bytes 2097152 | tf_op jit(solution)/shard_map/all_to_all | solution.py:103
  66.5 4.3 %fusion.14 = f32[1024,2048]{1,0:T(8,128)S(1)} fusion(bf16[1024,512]{1,0:T(8,128)(2,1)} %bitcast.4, bf16[1,512,2048]{2,1,0:T(8,128)(2,1)} %param.18), kind=kOutput, calls=%fused_computation.23 | convolution fusion | flops 2147483648 | bytes 11534336 | tf_op jit(solution)/shard_map/dot_general | solution.py:34
  70.8 3.2 %copy-done.6 = f32[1024,2048]{1,0:T(8,128)} copy-done((f32[1024,2048]{1,0:T(8,128)}, f32[1024,2048]{1,0:T(8,128)S(1)}, u32[]{:S(2)}) %copy-start.6) | copy-done | bytes 8388632
  74.0 4.0 %fusion.19 = bf16[1024,512]{1,0:T(8,128)(2,1)} fusion(bf16[1,2048,512]{2,1,0:T(8,128)(2,1)S(1)} %copy-done, f32[1024,2048]{1,0:T(8,128)S(1)} %fusion.14), kind=kOutput, calls=%fused_computation.26 | convolution fusion | flops 2166882304 | bytes 11534336 | tf_op jit(solution)/shard_map/dot_general | solution.py:37
  78.0 17.1 %all-to-all-done.2 = bf16[64,16,512]{2,1,0:T(8,128)(2,1)S(1)} async-done(((bf16[64,16,512]{2,1,0:T(8,128)(2,1)}), bf16[64,16,512]{2,1,0:T(8,128)(2,1)S(1)}, u32[]{:S(2)}, u32[]{:S(2)}) %all-to-all-start.2) | async-done | bytes 1048608 | tf_op jit(solution)/shard_map/all_to_all | solution.py:103
  96.0 6.2 %all-to-all-start.1 = ((bf16[64,16,512]{2,1,0:T(8,128)(2,1)}), bf16[64,16,512]{2,1,0:T(8,128)(2,1)S(1)}, u32[]{:S(2)}, u32[]{:S(2)}) async-start(bf16[64,16,512]{2,1,0:T(8,128)(2,1)} %bitcast.65), calls=%async_computation.1 | async-start | bytes 2097152 | tf_op jit(solution)/shard_map/all_to_all | solution.py:100
  102.2 8.8 %fusion.6 = bf16[1024,2048]{1,0:T(8,128)(2,1)S(1)} fusion(f32[1024,2048]{1,0:T(8,128)} %copy-done.6, bf16[1024,512]{1,0:T(8,128)(2,1)} %bitcast.67, bf16[1,2048,512]{2,1,0:T(8,128)(2,1)S(1)} %copy-done), kind=kOutput, calls=%fused_computation.12 | convolution fusion | flops 2187329536 | bytes 15728640 | tf_op jit(solution)/shard_map/dot_general | solution.py:28
  113.0 5.2 %fusion.7 = bf16[1,512,2048]{2,1,0:T(8,128)(2,1)} fusion(bf16[1024,512]{1,0:T(8,128)(2,1)} %bitcast.4, bf16[1024,2048]{1,0:T(8,128)(2,1)S(1)} %fusion.6), kind=kOutput, calls=%fused_computation.16 | convolution fusion | flops 2148532224 | bytes 7340032 | tf_op jit(solution)/shard_map/dot_general | solution.py:22
  118.2 4.3 %fusion.8 = bf16[1,2048,512]{2,1,0:T(8,128)(2,1)} fusion(bf16[1024,512]{1,0:T(8,128)(2,1)S(1)} %bitcast.68, f32[1024,2048]{1,0:T(8,128)S(1)} %copy-done.7), kind=kOutput, calls=%fused_computation.17 | convolution fusion | flops 2167406592 | bytes 11534336 | tf_op jit(solution)/shard_map/dot_general | solution.py:22
  122.5 6.2 %fusion.16 = bf16[1024,512]{1,0:T(8,128)(2,1)} fusion(bf16[1024,2048]{1,0:T(8,128)(2,1)} %copy-done.8, bf16[1,512,2048]{2,1,0:T(8,128)(2,1)} %param.18), kind=kOutput, calls=%fused_computation.25 | convolution fusion | flops 2148007936 | bytes 7340032 | tf_op jit(solution)/shard_map/dot_general | solution.py:28
  130.7 8.5 %all-to-all-start.3 = ((bf16[64,16,512]{2,1,0:T(8,128)(2,1)}), bf16[64,16,512]{2,1,0:T(8,128)(2,1)}, u32[]{:S(2)}, u32[]{:S(2)}) async-start(bf16[64,16,512]{2,1,0:T(8,128)(2,1)} %bitcast.66), calls=%async_computation.3 | async-start | bytes 2097152 | tf_op jit(solution)/shard_map/all_to_all | solution.py:108
  141.8 2.6 %gather_fusion = bf16[512,512]{1,0:T(8,128)(2,1)} fusion(bf16[1024,512]{1,0:T(8,128)(2,1)S(1)} %bitcast.64, s32[1024]{0:T(1024)S(1)} %pad_clamp_fusion), kind=kCustom, calls=%fused_computation | custom fusion | bytes 1050624 | tf_op jit(solution)/shard_map/gather | solution.py:111
  146.1 4.0 %multiply_reduce_fusion = (f32[256,2]{1,0:T(8,128)}, f32[256,512]{1,0:T(8,128)}) fusion(f32[256,2,512]{2,1,0:T(2,128)S(1)} %reshape.188, f32[256,512]{1,0:T(8,128)} %convert_element_type.80, f32[256,2]{1,0:T(8,128)S(1)} %copy.28), kind=kLoop, calls=%fused_computation.32 | loop fusion | flops 916992 | bytes 2101248 | tf_op jit(solution)/shard_map/reduce_sum | solution.py:121
  151.1 16.6 %all-to-all-done.3 = bf16[64,16,512]{2,1,0:T(8,128)(2,1)} async-done(((bf16[64,16,512]{2,1,0:T(8,128)(2,1)}), bf16[64,16,512]{2,1,0:T(8,128)(2,1)}, u32[]{:S(2)}, u32[]{:S(2)}) %all-to-all-start.3) | async-done | bytes 1048608 | tf_op jit(solution)/shard_map/all_to_all | solution.py:108
  167.7 4.0 %gather_fusion.1 = bf16[512,512]{1,0:T(8,128)(2,1)} fusion(bf16[1024,512]{1,0:T(8,128)(2,1)} %bitcast.12, s32[1024]{0:T(1024)S(1)} %pad_clamp_fusion), kind=kCustom, calls=%fused_computation.1 | custom fusion | bytes 1050624 | tf_op jit(solution)/shard_map/gather | solution.py:114
  173.4 2.1 reduce_sum.79
  178.1 2.2 fusion.23
  180.4 41.0 %all-reduce.3.cloned.1.call-done = (bf16[1,512,2048]{2,1,0:T(8,128)(2,1)}, bf16[1,2048,512]{2,1,0:T(8,128)(2,1)}) async-done(((bf16[1,512,2048]{2,1,0:T(8,128)(2,1)}, bf16[1,2048,512]{2,1,0:T(8,128)(2,1)}), (bf16[1,512,2048]{2,1,0:T(8,128)(2,1)}, bf16[1,2048,512]{2,1,0:T(8,128)(2,1)})) %all-reduce.3.cloned.1.call-update) | async-done | bytes 4194320 | tf_op jit(solution)/shard_map/psum | solution.py:48
  221.3 3.2 %copy.40 = bf16[1,512,2048]{2,1,0:T(8,128)(2,1)} copy(bf16[1,512,2048]{2,1,0:T(8,128)(2,1)} %get-tuple-element.12) | data formatting | bytes 4194304
  224.5 3.0 %copy.41 = bf16[1,2048,512]{2,1,0:T(8,128)(2,1)} copy(bf16[1,2048,512]{2,1,0:T(8,128)(2,1)} %get-tuple-element.13) | data formatting | bytes 4194304
  (55 shorter events, 27.9 us)
Async XLA Ops:
  7.2 66.8 %copy-start = (bf16[1,2048,512]{2,1,0:T(8,128)(2,1)S(1)}, bf16[1,2048,512]{2,1,0:T(8,128)(2,1)}, u32[]{:S(2)}) copy-start(bf16[1,2048,512]{2,1,0:T(8,128)(2,1)} %param.19) | copy-start | bytes 6291460
  15.0 55.7 %copy-start.5 = (s32[512,1]{0,1:T(1,128)}, s32[512,1]{0,1:T(1,128)S(1)}, u32[]{:S(2)}) copy-start(s32[512,1]{0,1:T(1,128)S(1)} %compare_select_fusion) | copy-start | bytes 6148
  18.5 41.8 %all-to-all-start = ((bf16[64,16,512]{2,1,0:T(8,128)(2,1)}), bf16[64,16,512]{2,1,0:T(8,128)(2,1)}, u32[]{:S(2)}, u32[]{:S(2)}) async-start(bf16[64,16,512]{2,1,0:T(8,128)(2,1)} %bitcast.3), calls=%async_computation | async-start | bytes 2097152 | tf_op jit(solution)/shard_map/all_to_all | solution.py:97
  60.3 34.7 %all-to-all-start.2 = ((bf16[64,16,512]{2,1,0:T(8,128)(2,1)}), bf16[64,16,512]{2,1,0:T(8,128)(2,1)S(1)}, u32[]{:S(2)}, u32[]{:S(2)}) async-start(bf16[64,16,512]{2,1,0:T(8,128)(2,1)} %bitcast.9), calls=%async_computation.2 | async-start | bytes 2097152 | tf_op jit(solution)/shard_map/all_to_all | solution.py:103
  70.8 3.2 %copy-start.6 = (f32[1024,2048]{1,0:T(8,128)}, f32[1024,2048]{1,0:T(8,128)S(1)}, u32[]{:S(2)}) copy-start(f32[1024,2048]{1,0:T(8,128)S(1)} %fusion.14) | copy-start | bytes 25165828
  95.0 1.0 copy-start.1
  96.0 34.7 %all-to-all-start.1 = ((bf16[64,16,512]{2,1,0:T(8,128)(2,1)}), bf16[64,16,512]{2,1,0:T(8,128)(2,1)S(1)}, u32[]{:S(2)}, u32[]{:S(2)}) async-start(bf16[64,16,512]{2,1,0:T(8,128)(2,1)} %bitcast.65), calls=%async_computation.1 | async-start | bytes 2097152 | tf_op jit(solution)/shard_map/all_to_all | solution.py:100
  102.2 119.2 %all-reduce.3.cloned.1.call-start = ((), (), s32[]{:S(2)}) async-start(), calls=%async_computation.4 | async-start | bytes 8388608 | tf_op jit(solution)/shard_map/psum | solution.py:48
  111.0 2.0 copy-start.8
  113.0 5.2 %copy-start.2 = (bf16[64,16,512]{2,1,0:T(8,128)(2,1)S(1)}, bf16[64,16,512]{2,1,0:T(8,128)(2,1)}, u32[]{:S(2)}) copy-start(bf16[64,16,512]{2,1,0:T(8,128)(2,1)} %copy-done.1) | copy-start | bytes 3145732
  113.0 5.2 %copy-start.7 = (f32[1024,2048]{1,0:T(8,128)S(1)}, f32[1024,2048]{1,0:T(8,128)}, u32[]{:S(2)}) copy-start(f32[1024,2048]{1,0:T(8,128)} %copy-done.6) | copy-start | bytes 25165828
  130.7 37.0 %all-to-all-start.3 = ((bf16[64,16,512]{2,1,0:T(8,128)(2,1)}), bf16[64,16,512]{2,1,0:T(8,128)(2,1)}, u32[]{:S(2)}, u32[]{:S(2)}) async-start(bf16[64,16,512]{2,1,0:T(8,128)(2,1)} %bitcast.66), calls=%async_computation.3 | async-start | bytes 2097152 | tf_op jit(solution)/shard_map/all_to_all | solution.py:108
  141.1 35.2 %copy-start.4 = (s32[256,2]{0,1:T(2,128)S(1)}, s32[256,2]{0,1:T(2,128)}, u32[]{:S(2)}) copy-start(s32[256,2]{0,1:T(2,128)} %param.12) | copy-start | bytes 6148
  150.1 28.1 %copy-start.3 = (bf16[512,64]{0,1:T(8,128)(2,1)S(1)}, bf16[512,64]{0,1:T(8,128)(2,1)}, u32[]{:S(2)}) copy-start(bf16[512,64]{0,1:T(8,128)(2,1)} %param.17) | copy-start | bytes 196612
Sparse Core Ops, SparseCore 0:
  122.6 98.6 all-reduce.2
where the time goes:
time: 236 us; the launch traced here: 234 us
  waiting for transfers between devices  95.2 us (40%)
  matrix products  39.4 us (17%)
  starting transfers between devices  34.3 us (15%)
  local copies, waits for them, and re-layouts  32.2 us (14%)
  other arithmetic  19 us (8%)
  between operations  14.2 us (6%)
    psum x1, waiting for transfers between devices, expert_backward(): lax.psum(grad_up_part.astype(jnp.bfloat16), 'dp').astype(jnp.float32)  41 us
    all_to_all x1, waiting for transfers between devices, per_device(): lax.all_to_all(send_in, 'expert', split_axis=0, concat_axis=0, tiled=True)  18.6 us
    all_to_all x1, waiting for transfers between devices, per_device(): lax.all_to_all(send_cot, 'expert', split_axis=0, concat_axis=0, tiled=True)  17.1 us
    all_to_all x1, waiting for transfers between devices, per_device(): lax.all_to_all(d_inputs.reshape(buffer_shape), 'expert', split_axis=0, co...  16.6 us
    dot_general x2, matrix products, contract_cols(): lax.dot_general(left, right, (((1,), (1,)), ((), ())), preferred_element_...  15 us
    all_to_all x1, starting transfers between devices, per_device(): lax.all_to_all(send_in, 'expert', split_axis=0, concat_axis=0, tiled=True)  13.3 us
    unnamed x21, local copies, waits for them, and re-layouts  13.2 us
    dot_general x2, matrix products, contract_rows(): lax.dot_general(left, right, (((0,), (0,)), ((), ())), preferred_element_...  9.5 us
  transfers between devices with their start and end apart: 5, of which 5 were waited for; matrix products, arithmetic and copies ran while one was open for 29% of the time, Pallas kernels for 0%

commit v1 on v0

--- a/solution.py
+++ b/solution.py
@@ -6,6 +6,11 @@
 TOP = 2
 coef_a = 0.7978845608028654
 coef_b = 0.044715
+
+
+def series_divide(frame):
+    long_array = lax.all_gather(frame, axis_name="dp").sum(axis=0)
+    return long_array
 
 
 def gelu_pair(pre_act):
@@ -45,7 +50,7 @@
     d_inputs = contract_cols(d_pre, w_up_one).astype(jnp.bfloat16)
     grad_up_part = contract_rows(flat_in, d_pre)
     sum_up, sum_down = (
-        lax.psum(grad_up_part.astype(jnp.bfloat16), "dp").astype(jnp.float32),
+        series_divide(grad_up_part.astype(jnp.bfloat16)).astype(jnp.float32),
         lax.psum(grad_down_part.astype(jnp.bfloat16), "dp").astype(jnp.float32),
     )
     return (d_inputs, sum_up, sum_down)

time: 236 us -> 273 us (1.16)
  waiting for transfers between devices: 95.2 us -> 120 us
  matrix products: 39.4 us -> 50.4 us
  other arithmetic: 19 us -> 26.3 us
  local copies, waits for them, and re-layouts: 32.2 us -> 28 us
    all_to_all x1, waiting for transfers between devices: 1.98 us -> 21.9 us  [per_device(): lax.all_to_all(outputs.reshape(buffer_shape), 'expert', split_axis=0, con...]
    psum x1, waiting for transfers between devices: 41 us -> 53.3 us  [expert_backward(): lax.psum(grad_down_part.astype(jnp.bfloat16), 'dp').astype(jnp.float32)]
    all_to_all x1, waiting for transfers between devices: 16.6 us -> 5.37 us  [per_device(): lax.all_to_all(d_inputs.reshape(buffer_shape), 'expert', split_axis=0, co...]
    reduce_sum x0 -> x1, other arithmetic: none -> 7.2 us  [series_divide(): long_array = lax.all_gather(frame, axis_name='dp').sum(axis=0)]
    unnamed x21 -> x16, local copies, waits for them, and re-layouts: 13.2 us -> 6.76 us
    dot_general x2, matrix products: 9.5 us -> 13.7 us  [contract_rows(): lax.dot_general(left, right, (((0,), (0,)), ((), ())), preferred_element_...]
    all_to_all x1, waiting for transfers between devices: 17.1 us -> 20.8 us  [per_device(): lax.all_to_all(send_cot, 'expert', split_axis=0, concat_axis=0, tiled=True)]
    dot_general x1, matrix products: 4.26 us -> 7.47 us  [expert_forward(): pre_act = jnp.dot(flat_in, w_up_one, preferred_element_type=jnp.float32)]
  transfers between devices with their start and end apart: 5 -> 6, of which waited for: 5 -> 5; matrix products, arithmetic and copies ran while one was open for 29% -> 27% of each run, Pallas kernels for 0% -> 0%
where the time goes in v1:
time: 273 us; the launch traced here: 271 us
  waiting for transfers between devices  120 us (44%)
  matrix products  50.4 us (18%)
  starting transfers between devices  32.4 us (12%)
  local copies, waits for them, and re-layouts  28 us (10%)
  other arithmetic  26.3 us (10%)
  between operations  14.2 us (5%)
    psum x1, waiting for transfers between devices, expert_backward(): lax.psum(grad_down_part.astype(jnp.bfloat16), 'dp').astype(jnp.float32)  53.3 us
    all_to_all x1, waiting for transfers between devices, per_device(): lax.all_to_all(outputs.reshape(buffer_shape), 'expert', split_axis=0, con...  21.9 us
    all_to_all x1, waiting for transfers between devices, per_device(): lax.all_to_all(send_cot, 'expert', split_axis=0, concat_axis=0, tiled=True)  20.8 us
    all_to_all x1, waiting for transfers between devices, per_device(): lax.all_to_all(send_in, 'expert', split_axis=0, concat_axis=0, tiled=True)  18.6 us
    dot_general x2, matrix products, contract_cols(): lax.dot_general(left, right, (((1,), (1,)), ((), ())), preferred_element_...  15.3 us
    dot_general x2, matrix products, contract_rows(): lax.dot_general(left, right, (((0,), (0,)), ((), ())), preferred_element_...  13.7 us
    all_to_all x1, starting transfers between devices, per_device(): lax.all_to_all(send_in, 'expert', split_axis=0, concat_axis=0, tiled=True)  13.3 us
    dot_general x1, matrix products, expert_forward(): pre_act = jnp.dot(flat_in, w_up_one, preferred_element_type=jnp.float32)  7.47 us
  transfers between devices with their start and end apart: 6, of which 5 were waited for; matrix products, arithmetic and copies ran while one was open for 27% of the time, Pallas kernels for 0%

profile of v1, /device:TPU:1, one launch (start us, length us, event | category | flops | bytes accessed | tf_op | source)
XLA Modules:
  0.0 271.3 jit_solution(18171868954820905938)
XLA Ops:
  15.8 4.0 %scatter_custom_fusion = bf16[1024,512]{1,0:T(8,128)(2,1)} fusion(s32[512]{0:T(512)S(1)} %bitcast.73, bf16[512,512]{1,0:T(8,128)(2,1)} %reshape.212, bf16[]{:T(256)} %constant.12.clone.1), kind=kCustom, calls=%fused_computation.38 | custom fusion | bytes 1049088 | tf_op jit(solution)/shard_map/scatter | solution.py:91
  19.8 13.3 %all-to-all-start = ((bf16[64,16,512]{2,1,0:T(8,128)(2,1)}), bf16[64,16,512]{2,1,0:T(8,128)(2,1)}, u32[]{:S(2)}, u32[]{:S(2)}) async-start(bf16[64,16,512]{2,1,0:T(8,128)(2,1)} %bitcast.3), calls=%async_computation | async-start | bytes 2097152 | tf_op jit(solution)/shard_map/all_to_all | solution.py:102
  38.7 4.2 %scatter_custom_fusion.1 = bf16[1024,512]{1,0:T(8,128)(2,1)} fusion(s32[512]{0:T(512)S(1)} %bitcast.74, f32[512,512]{1,0:T(8,128)} %mul.134, f32[512]{0:T(512)S(1)} %reshape.190, bf16[]{:T(256)} %constant.12.clone.1), kind=kCustom, calls=%fused_computation.34 | custom fusion | flops 524288 | bytes 2099202 | tf_op jit(solution)/shard_map/scatter | solution.py:97
  42.9 18.6 %all-to-all-done = bf16[64,16,512]{2,1,0:T(8,128)(2,1)} async-done(((bf16[64,16,512]{2,1,0:T(8,128)(2,1)}), bf16[64,16,512]{2,1,0:T(8,128)(2,1)}, u32[]{:S(2)}, u32[]{:S(2)}) %all-to-all-start) | async-done | bytes 1048608 | tf_op jit(solution)/shard_map/all_to_all | solution.py:102
  61.6 6.2 %all-to-all-start.2 = ((bf16[64,16,512]{2,1,0:T(8,128)(2,1)}), bf16[64,16,512]{2,1,0:T(8,128)(2,1)S(1)}, u32[]{:S(2)}, u32[]{:S(2)}) async-start(bf16[64,16,512]{2,1,0:T(8,128)(2,1)} %bitcast.9), calls=%async_computation.2 | async-start | bytes 2097152 | tf_op jit(solution)/shard_map/all_to_all | solution.py:108
  68.0 7.5 %fusion.13 = f32[1024,2048]{1,0:T(8,128)} fusion(bf16[1024,512]{1,0:T(8,128)(2,1)} %bitcast.4, bf16[1,512,2048]{2,1,0:T(8,128)(2,1)} %param.18), kind=kOutput, calls=%fused_computation.22 | convolution fusion | flops 2147483648 | bytes 11534336 | tf_op jit(solution)/shard_map/dot_general | solution.py:39
  75.5 20.8 %all-to-all-done.2 = bf16[64,16,512]{2,1,0:T(8,128)(2,1)S(1)} async-done(((bf16[64,16,512]{2,1,0:T(8,128)(2,1)}), bf16[64,16,512]{2,1,0:T(8,128)(2,1)S(1)}, u32[]{:S(2)}, u32[]{:S(2)}) %all-to-all-start.2) | async-done | bytes 1048608 | tf_op jit(solution)/shard_map/all_to_all | solution.py:108
  96.3 8.6 %fusion.6 = bf16[1024,2048]{1,0:T(8,128)(2,1)S(1)} fusion(f32[1024,2048]{1,0:T(8,128)} %fusion.13, bf16[1024,512]{1,0:T(8,128)(2,1)S(1)} %bitcast.68, bf16[1,2048,512]{2,1,0:T(8,128)(2,1)S(1)} %copy-done), kind=kOutput, calls=%fused_computation.12 | convolution fusion | flops 2187329536 | bytes 15728640 | tf_op jit(solution)/shard_map/dot_general | solution.py:33
  106.9 5.0 %convolution_convert_fusion.1 = bf16[512,2048]{1,0:T(8,128)(2,1)} fusion(bf16[1024,512]{1,0:T(8,128)(2,1)} %bitcast.4, bf16[1024,2048]{1,0:T(8,128)(2,1)S(1)} %fusion.6), kind=kOutput, calls=%fused_computation.15 | convolution fusion | flops 2148532224 | bytes 7340032 | tf_op jit(solution)/shard_map/dot_general | solution.py:27
  111.9 7.1 %fusion.18 = bf16[1024,512]{1,0:T(8,128)(2,1)} fusion(bf16[1,2048,512]{2,1,0:T(8,128)(2,1)S(1)} %copy-done, f32[1024,2048]{1,0:T(8,128)} %fusion.13), kind=kOutput, calls=%fused_computation.25 | convolution fusion | flops 2166882304 | bytes 11534336 | tf_op jit(solution)/shard_map/dot_general | solution.py:42
  119.0 6.2 %all-to-all-start.1 = ((bf16[64,16,512]{2,1,0:T(8,128)(2,1)}), bf16[64,16,512]{2,1,0:T(8,128)(2,1)S(1)}, u32[]{:S(2)}, u32[]{:S(2)}) async-start(bf16[64,16,512]{2,1,0:T(8,128)(2,1)} %bitcast.71), calls=%async_computation.1 | async-start | bytes 2097152 | tf_op jit(solution)/shard_map/all_to_all | solution.py:105
  125.2 6.7 %fusion.15 = bf16[1024,512]{1,0:T(8,128)(2,1)} fusion(bf16[1024,2048]{1,0:T(8,128)(2,1)} %copy-done.6, bf16[1,512,2048]{2,1,0:T(8,128)(2,1)} %param.18), kind=kOutput, calls=%fused_computation.24 | convolution fusion | flops 2148007936 | bytes 7340032 | tf_op jit(solution)/shard_map/dot_general | solution.py:33
  131.9 21.9 %all-to-all-done.1 = bf16[64,16,512]{2,1,0:T(8,128)(2,1)S(1)} async-done(((bf16[64,16,512]{2,1,0:T(8,128)(2,1)}), bf16[64,16,512]{2,1,0:T(8,128)(2,1)S(1)}, u32[]{:S(2)}, u32[]{:S(2)}) %all-to-all-start.1) | async-done | bytes 1048608 | tf_op jit(solution)/shard_map/all_to_all | solution.py:105
  154.7 6.4 %all-to-all-start.3 = ((bf16[64,16,512]{2,1,0:T(8,128)(2,1)}), bf16[64,16,512]{2,1,0:T(8,128)(2,1)S(1)}, u32[]{:S(2)}, u32[]{:S(2)}) async-start(bf16[64,16,512]{2,1,0:T(8,128)(2,1)} %bitcast.70), calls=%async_computation.3 | async-start | bytes 2097152 | tf_op jit(solution)/shard_map/all_to_all | solution.py:113
  161.2 8.7 %fusion.7 = bf16[1,2048,512]{2,1,0:T(8,128)(2,1)} fusion(bf16[1024,512]{1,0:T(8,128)(2,1)} %bitcast.69, f32[1024,2048]{1,0:T(8,128)} %fusion.13), kind=kOutput, calls=%fused_computation.16 | convolution fusion | flops 2167406592 | bytes 11534336 | tf_op jit(solution)/shard_map/dot_general | solution.py:27
  172.4 4.0 %gather_fusion = bf16[512,512]{1,0:T(8,128)(2,1)} fusion(bf16[1024,512]{1,0:T(8,128)(2,1)} %bitcast.65, s32[1024]{0:T(1024)S(1)} %pad_clamp_fusion), kind=kCustom, calls=%fused_computation | custom fusion | bytes 1050624 | tf_op jit(solution)/shard_map/gather | solution.py:116
  176.5 2.7 reshape.188
  179.1 4.1 %multiply_reduce_fusion = (f32[256,2]{1,0:T(8,128)}, f32[256,512]{1,0:T(8,128)}) fusion(f32[256,2,512]{2,1,0:T(2,128)} %reshape.188, f32[256,512]{1,0:T(8,128)} %convert_element_type.82, f32[256,2]{1,0:T(8,128)S(1)} %copy.28), kind=kLoop, calls=%fused_computation.31 | loop fusion | flops 916992 | bytes 2101248 | tf_op jit(solution)/shard_map/reduce_sum | solution.py:126
  184.3 5.4 %all-to-all-done.3 = bf16[64,16,512]{2,1,0:T(8,128)(2,1)S(1)} async-done(((bf16[64,16,512]{2,1,0:T(8,128)(2,1)}), bf16[64,16,512]{2,1,0:T(8,128)(2,1)S(1)}, u32[]{:S(2)}, u32[]{:S(2)}) %all-to-all-start.3) | async-done | bytes 1048608 | tf_op jit(solution)/shard_map/all_to_all | solution.py:113
  189.7 2.6 gather_fusion.1
  198.7 2.2 fusion.22
  200.9 7.2 %reduce_sum.95 = bf16[512,2048]{1,0:T(8,128)(2,1)} reduce(bf16[4,512,2048]{2,1,0:T(8,128)(2,1)} %bitcast.66, bf16[]{:T(256)} %constant.12.clone.1), dimensions={0}, to_apply=%region_12.13 | reduce | flops 3145728 | bytes 10485762 | tf_op jit(solution)/shard_map/reduce_sum | solution.py:12
  208.1 53.3 %all-reduce.2.cloned.1.call-done = bf16[1,2048,512]{2,1,0:T(8,128)(2,1)} async-done(((bf16[1,2048,512]{2,1,0:T(8,128)(2,1)}), bf16[1,2048,512]{2,1,0:T(8,128)(2,1)}) %all-reduce.2.cloned.1.call-update) | async-done | bytes 2097168 | tf_op jit(solution)/shard_map/psum | solution.py:54
  261.4 3.0 %copy.39 = bf16[1,2048,512]{2,1,0:T(8,128)(2,1)} copy(bf16[1,2048,512]{2,1,0:T(8,128)(2,1)} %all-reduce.2.cloned.1.call-done) | data formatting | bytes 4194304
  (54 shorter events, 27.2 us)
Async XLA Ops:
  7.2 89.1 %copy-start = (bf16[1,2048,512]{2,1,0:T(8,128)(2,1)S(1)}, bf16[1,2048,512]{2,1,0:T(8,128)(2,1)}, u32[]{:S(2)}) copy-start(bf16[1,2048,512]{2,1,0:T(8,128)(2,1)} %param.19) | copy-start | bytes 6291460
  15.8 59.7 %copy-start.5 = (s32[512,1]{0,1:T(1,128)}, s32[512,1]{0,1:T(1,128)S(1)}, u32[]{:S(2)}) copy-start(s32[512,1]{0,1:T(1,128)S(1)} %compare_select_fusion) | copy-start | bytes 6148
  19.8 41.8 %all-to-all-start = ((bf16[64,16,512]{2,1,0:T(8,128)(2,1)}), bf16[64,16,512]{2,1,0:T(8,128)(2,1)}, u32[]{:S(2)}, u32[]{:S(2)}) async-start(bf16[64,16,512]{2,1,0:T(8,128)(2,1)} %bitcast.3), calls=%async_computation | async-start | bytes 2097152 | tf_op jit(solution)/shard_map/all_to_all | solution.py:102
  61.6 34.7 %all-to-all-start.2 = ((bf16[64,16,512]{2,1,0:T(8,128)(2,1)}), bf16[64,16,512]{2,1,0:T(8,128)(2,1)S(1)}, u32[]{:S(2)}, u32[]{:S(2)}) async-start(bf16[64,16,512]{2,1,0:T(8,128)(2,1)} %bitcast.9), calls=%async_computation.2 | async-start | bytes 2097152 | tf_op jit(solution)/shard_map/all_to_all | solution.py:108
  67.8 133.2 %all-gather.3.cloned.1.call-start = ((), (), s32[]{:S(2)}) async-start(), calls=%async_computation.5 | async-start | bytes 10485760 | tf_op jit(solution)/shard_map/all_gather | solution.py:12
  96.3 8.7 %copy-start.2 = (bf16[64,16,512]{2,1,0:T(8,128)(2,1)}, bf16[64,16,512]{2,1,0:T(8,128)(2,1)S(1)}, u32[]{:S(2)}) copy-start(bf16[64,16,512]{2,1,0:T(8,128)(2,1)S(1)} %all-to-all-done.2) | copy-start | bytes 3145732
  104.9 1.9 copy-start.6
  119.0 34.7 %all-to-all-start.1 = ((bf16[64,16,512]{2,1,0:T(8,128)(2,1)}), bf16[64,16,512]{2,1,0:T(8,128)(2,1)S(1)}, u32[]{:S(2)}, u32[]{:S(2)}) async-start(bf16[64,16,512]{2,1,0:T(8,128)(2,1)} %bitcast.71), calls=%async_computation.1 | async-start | bytes 2097152 | tf_op jit(solution)/shard_map/all_to_all | solution.py:105
  153.7 1.0 copy-start.1
  154.7 35.0 %all-to-all-start.3 = ((bf16[64,16,512]{2,1,0:T(8,128)(2,1)}), bf16[64,16,512]{2,1,0:T(8,128)(2,1)S(1)}, u32[]{:S(2)}, u32[]{:S(2)}) async-start(bf16[64,16,512]{2,1,0:T(8,128)(2,1)} %bitcast.70), calls=%async_computation.3 | async-start | bytes 2097152 | tf_op jit(solution)/shard_map/all_to_all | solution.py:113
  161.1 100.3 %all-reduce.2.cloned.1.call-start = ((), (), s32[]{:S(2)}) async-start(), calls=%async_computation.4 | async-start | bytes 4194304 | tf_op jit(solution)/shard_map/psum | solution.py:54
  171.7 25.1 %copy-start.4 = (s32[256,2]{0,1:T(2,128)S(1)}, s32[256,2]{0,1:T(2,128)}, u32[]{:S(2)}) copy-start(s32[256,2]{0,1:T(2,128)} %param.12) | copy-start | bytes 6148
  183.3 15.4 %copy-start.3 = (bf16[512,64]{0,1:T(8,128)(2,1)S(1)}, bf16[512,64]{0,1:T(8,128)(2,1)}, u32[]{:S(2)}) copy-start(bf16[512,64]{0,1:T(8,128)(2,1)} %param.17) | copy-start | bytes 196612
Sparse Core Ops, SparseCore 0:
  112.0 82.2 all-gather.2
  196.7 64.7 all-reduce.1
